TPU v7x, 32 devices: a whole 2x2x4 slice. The times are simulated.
32 devices in a mesh: test: 4 (over z), cell: 8 (over y, x, core).
Axes of the slice: x: 2, y: 2, z: 4, core: 2. Of those that a mesh axis runs over, the one named last changes fastest.
Arguments:
- log_perm: float32 [128, 16, 256], P('cell'), may hold values from -1 to 1
- panel: float32 [8, 128, 16, 256], P('test', 'cell'), may hold values from -4 to 4
- wells: int32 [4, 8], P('test'), may hold values from 0 to 524287
- rates: float32 [4, 8], P('test'), may hold values from 1 to 10
- recharge: float32 [4, 128, 16, 256], P('test', 'cell'), may hold values from 0.25 to 4
- gauge: float32 [128, 16, 256], P('cell'), may hold values from 0.25 to 4
Outputs:
- hessian_panel: float32 [8, 128, 16, 256], P('test', 'cell')
Inputs may be any that keep to these rules, and one draw needn't show every extreme that they name: `wells`: each entry names a cell of the whole grid, numbered x * 16 * 256 + y * 256 + z; a test may name a cell more than once.
All inputs are finite; a program needn't handle non-finite values.
Results may differ from a plain program's by a relative error of at most 0.0001.
Values sent between devices are 32-bit elements; how exact they have to be, the bound alone decides.
No kernel may reach another device: no remote copies, remote signals or barrier semaphores. Data moves between devices by JAX's collectives and lax.ppermute only.
A program may use at most 64 MiB of HBM per device.

v0:
```python
import math
import jax
import jax.numpy as jnp
import numpy as np
from jax import lax
from jax.sharding import PartitionSpec as P

CHEB = 4
storage = 0.02


def with_halo(cells, sides, width):
    for axis, dim in sides:
        count = lax.axis_size(axis)
        ends = count - 1
        head = lax.slice_in_dim(cells, 0, width, axis=dim)
        tail = lax.slice_in_dim(cells, cells.shape[dim] - width, cells.shape[dim], axis=dim)
        cells = jnp.concatenate(
            [
                lax.ppermute(tail, axis, [(i, (i + 1) % count) for i in range(ends)]),
                cells,
                lax.ppermute(head, axis, [((i + 1) % count, i) for i in range(ends)]),
            ],
            axis=dim,
        )
    return cells


def cheb_table(count):
    highest = storage + 12.0 * math.e
    theta = 0.5 * (highest + storage)
    spread = 0.5 * (highest - storage)
    sigma = theta / spread
    rho = 1.0 / sigma
    keeps = []
    pushes = []
    for turn in range(count):
        after = 1.0 / (2.0 * sigma - rho)
        keeps.append(after * rho)
        pushes.append(2.0 * after / spread)
        rho = after
    return (1.0 / theta, keeps, pushes)


def neighbours(field, back):
    axis = field.ndim - back
    widths = [(0, 0)] * field.ndim
    widths[axis] = (1, 1)
    padded = jnp.pad(field, widths)
    length = field.shape[axis]
    return (
        lax.slice_in_dim(padded, 2, length + 2, axis=axis),
        lax.slice_in_dim(padded, 0, length, axis=axis),
    )


def diffuse(weight_ext, field_ext):
    weight = weight_ext[..., 1:-1, :, :]
    field = field_ext[..., 1:-1, :, :]
    total = 0.5 * (weight + weight_ext[..., 2:, :, :]) * (field - field_ext[..., 2:, :, :])
    total = total + 0.5 * (weight + weight_ext[..., :-2, :, :]) * (
        field - field_ext[..., :-2, :, :]
    )
    for back in (2, 1):
        weight_up, weight_down = neighbours(weight, back)
        field_up, field_down = neighbours(field, back)
        total = (
            total
            + 0.5 * (weight + weight_up) * (field - field_up)
            + 0.5 * (weight + weight_down) * (field - field_down)
        )
    return total


def pairs(left_ext, right_ext):
    left = left_ext[..., 1:-1, :, :]
    right = right_ext[..., 1:-1, :, :]
    total = (left - left_ext[..., 2:, :, :]) * (right - right_ext[..., 2:, :, :])
    total = total + (left - left_ext[..., :-2, :, :]) * (right - right_ext[..., :-2, :, :])
    for back in (2, 1):
        left_up, left_down = neighbours(left, back)
        right_up, right_down = neighbours(right, back)
        total = (
            total
            + (left - left_up) * (right - right_up)
            + (left - left_down) * (right - right_down)
        )
    return total


def rims(field):
    return with_halo(field, (("cell", 1),), 1)


def shards(log_perm, panel, wells, rates, recharge, gauge):
    place = lax.axis_index("cell")
    slab, rows_y, depth_z = log_perm.shape
    tests_here, well_count = wells.shape
    first, keeps, pushes = cheb_table(CHEB)
    keep_table = jnp.asarray(np.array(keeps, np.float32))
    push_table = jnp.asarray(np.array(pushes, np.float32))
    columns = lax.all_gather(panel, "test", axis=0, tiled=True)
    columns_all = columns.shape[0]
    perm = jnp.exp(log_perm)
    stacked = jnp.concatenate([perm[None], perm[None] * columns], axis=0)
    coeff_ext = with_halo(stacked, (("cell", 1),), 2)
    perm_ext = coeff_ext[0]
    scaled_ext = coeff_ext[1:, 1:-1]
    cells = slab * rows_y * depth_z
    flat = place * cells + jnp.arange(cells, dtype=jnp.int32)
    hits = wells[:, :, None] == flat[None, None, :]
    points = jnp.sum(jnp.where(hits, rates[:, :, None], 0.0), axis=1).reshape(
        tests_here, slab, rows_y, depth_z
    )
    counts = jnp.sum(hits.astype(jnp.float32), axis=1).reshape(tests_here, slab, rows_y, depth_z)
    source = recharge + points
    observe = gauge[None] + counts

    def solve(right_side):
        solution = jnp.zeros_like(right_side)
        residual = right_side
        direction = right_side * first

        def sweep(turn, carry):
            solution, residual, direction = carry
            extended = with_halo(direction, (("cell", 1),), 1)
            image = storage * direction + diffuse(perm_ext[1:-1], extended)
            solution = solution + direction
            residual = residual - image
            direction = keep_table[turn] * direction + push_table[turn] * residual
            return (solution, residual, direction)

        solution, residual, direction = lax.fori_loop(
            0, CHEB, sweep, (solution, residual, direction)
        )
        return solution + direction

    state = solve(source)
    state_ext = rims(state)
    forcing = -diffuse(scaled_ext, state_ext[:, None])
    forcing = forcing.reshape(tests_here * columns_all, slab, rows_y, depth_z)
    change = solve(forcing)
    weighted = (
        change.reshape(tests_here, columns_all, slab, rows_y, depth_z) * observe[:, None]
    ).reshape(tests_here * columns_all, slab, rows_y, depth_z)
    adjoint = solve(weighted)
    adjoint_ext = rims(adjoint).reshape(tests_here, columns_all, slab + 2, rows_y, depth_z)
    contrib = jnp.sum(pairs(state_ext[:, None], adjoint_ext), axis=0)
    partial_value = -0.5 * perm[None] * contrib
    total = lax.psum(partial_value, "test")
    share = panel.shape[0]
    owned = lax.dynamic_slice_in_dim(total, lax.axis_index("test") * share, share, 0)
    return owned


def solution(mesh):
    return jax.shard_map(
        shards,
        mesh=mesh,
        in_specs=(
            P("cell", None, None),
            P("test", "cell", None, None),
            P("test", None),
            P("test", None),
            P("test", "cell", None, None),
            P("cell", None, None),
        ),
        out_specs=P("test", "cell", None, None),
        check_vma=False,
    )
```

profile of v0, /device:TPU:0, one launch (start us, length us, event | category | flops | bytes accessed | tf_op | source)
XLA Modules:
  0.0 408.5 jit_solution(683576134354521020)
XLA Ops:
  7.3 1.7 broadcast_multiply_fusion.14
  9.1 48.2 %all-gather.2.cloned.1.call-done = f32[8,16,16,256]{3,2,1,0:T(8,128)} async-done(((f32[2,16,16,256]{3,2,1,0:T(8,128)}), f32[8,16,16,256]{3,2,1,0:T(8,128)}) %all-gather.2.cloned.1.call-update) | async-done | bytes 2097168 | tf_op jit(solution)/shard_map/all_gather | solution.py:102
  57.3 2.0 broadcast_multiply_fusion.6
  60.2 1.3 collective-permute-start.6
  61.4 3.0 collective-permute-start.7
  64.5 1.7 fusion.86
  66.3 1.8 broadcast_multiply_fusion.13
  70.8 51.1 %while.63 = (s32[]{:T(128)}, f32[1,16,16,256]{3,2,1,0:T(8,128)}, f32[1,16,16,256]{3,2,1,0:T(8,128)}, f32[1,16,16,256]{3,2,1,0:T(8,128)}, f32[16,16,256]{2,1,0:T(...) while((s32[]{:T(128)}, f32[1,16,16,256]{3,2,1,0:T(8,128)}, ...), condition=%wide.region_2.3_spmd.clone.clone, body=%wide.region_1.2_spmd.sunk.clone.clone.sunk | while | flops 2424835 | bytes 3637479 | solution.py:133
  71.7 3.3 collective-permute-start
  75.0 1.3 collective-permute-start.1
  77.6 2.4 collective-permute-done.1
  80.0 3.5 multiply_add_fusion.6
  84.4 4.4 %collective-permute-start = (f32[1,1,16,256]{3,2,1,0:T(8,128)S(1)}, f32[1,1,16,256]{3,2,1,0:T(8,128)S(1)}, u32[]{:S(2)}, u32[]{:S(2)}) collective-permute-start(f32[1,1,16,256]{3,2,1,0:T(8,128)S(1)} %get-tuple-element.979), channel_id=1, source_target_pairs={{0,1},{1,2},{2,3},{3,4},{4,5},{5,6},{6,7},{8,9},{9,10},{10,11},{11... | collective-permute-start | bytes 49160 | tf_op jit(solution)/shard_map/while/body/eval_jaxpr/ppermute | solution.py:20
  88.8 1.3 collective-permute-start.1
  92.1 3.6 multiply_add_fusion.6
  96.7 6.0 %collective-permute-start = (f32[1,1,16,256]{3,2,1,0:T(8,128)S(1)}, f32[1,1,16,256]{3,2,1,0:T(8,128)S(1)}, u32[]{:S(2)}, u32[]{:S(2)}) collective-permute-start(f32[1,1,16,256]{3,2,1,0:T(8,128)S(1)} %get-tuple-element.979), channel_id=1, source_target_pairs={{0,1},{1,2},{2,3},{3,4},{4,5},{5,6},{6,7},{8,9},{9,10},{10,11},{11... | collective-permute-start | bytes 49160 | tf_op jit(solution)/shard_map/while/body/eval_jaxpr/ppermute | solution.py:20
  102.7 1.3 collective-permute-start.1
  105.8 3.6 multiply_add_fusion.6
  110.3 4.8 %collective-permute-start = (f32[1,1,16,256]{3,2,1,0:T(8,128)S(1)}, f32[1,1,16,256]{3,2,1,0:T(8,128)S(1)}, u32[]{:S(2)}, u32[]{:S(2)}) collective-permute-start(f32[1,1,16,256]{3,2,1,0:T(8,128)S(1)} %get-tuple-element.979), channel_id=1, source_target_pairs={{0,1},{1,2},{2,3},{3,4},{4,5},{5,6},{6,7},{8,9},{9,10},{10,11},{11... | collective-permute-start | bytes 49160 | tf_op jit(solution)/shard_map/while/body/eval_jaxpr/ppermute | solution.py:20
  115.2 1.3 collective-permute-start.1
  118.2 3.6 multiply_add_fusion.6
  122.9 4.8 %collective-permute-start.8 = (f32[1,1,16,256]{3,2,1,0:T(8,128)S(1)}, f32[1,1,16,256]{3,2,1,0:T(8,128)S(1)}, u32[]{:S(2)}, u32[]{:S(2)}) collective-permute-start(f32[1,1,16,256]{3,2,1,0:T(8,128)S(1)} %get-tuple-element.831), channel_id=1, source_target_pairs={{0,1},{1,2},{2,3},{3,4},{4,5},{5,6},{6,7},{8,9},{9,10},{10,11},{11... | collective-permute-start | bytes 49160 | tf_op jit(solution)/shard_map/ppermute | solution.py:20
  127.7 1.3 collective-permute-start.9
  130.1 1.7 add.631
  131.9 1.4 broadcast_multiply_fusion.10
  133.3 4.0 broadcast_multiply_fusion.5
  137.3 76.5 %while.64 = (s32[]{:T(128)}, f32[8,16,16,256]{3,2,1,0:T(8,128)}, f32[8,16,16,256]{3,2,1,0:T(8,128)}, f32[8,16,16,256]{3,2,1,0:T(8,128)}, f32[16,16,256]{2,1,0:T(...) while((s32[]{:T(128)}, f32[8,16,16,256]{3,2,1,0:T(8,128)}, ...), condition=%wide.region_4.5_spmd.clone.clone, body=%wide.region_3.4_spmd.sunk.clone.clone.sunk | while | flops 14811139 | bytes 23068904 | solution.py:133
  137.3 1.6 copy.50
  139.6 4.5 %collective-permute-start.2 = (f32[8,1,16,256]{3,2,1,0:T(8,128)}, f32[8,1,16,256]{3,2,1,0:T(8,128)}, u32[]{:S(2)}, u32[]{:S(2)}) collective-permute-start(f32[8,1,16,256]{3,2,1,0:T(8,128)} %get-tuple-element.995), channel_id=1, source_target_pairs={{0,1},{1,2},{2,3},{3,4},{4,5},{5,6},{6,7},{8,9},{9,10},{10,11},{11... | collective-permute-start | bytes 393224 | tf_op jit(solution)/shard_map/while/body/eval_jaxpr/ppermute | solution.py:20
  144.0 1.3 collective-permute-start.3
  147.8 7.1 %multiply_add_fusion.7 = (f32[8,16,16,256]{3,2,1,0:T(8,128)}, f32[8,16,16,256]{3,2,1,0:T(8,128)}, f32[8,16,16,256]{3,2,1,0:T(8,128)}) fusion(f32[8,16,16,256]{3,2,1,0:T(8,128)S(1)} %copy.50, f32[]{:T(128)} %bitcast.98, f32[]{:T(128)} %bitcast.99, f32[8,16,16,256]{3,2,1,0:T(8,128)} %get-tuple-element.1066, f32[16,16,256]{2,1,0:T(8,128)S(1)} %get-tuple-element.991, ...), kind=kLoop, calls=%fused_computation.69.clone.1 | loop fusion | flops 14155776 | bytes 14417929 | tf_op jit(solution)/shard_map/while/body/eval_jaxpr/add | solution.py:130
  154.9 1.6 copy.50
  157.3 6.1 %collective-permute-start.2 = (f32[8,1,16,256]{3,2,1,0:T(8,128)}, f32[8,1,16,256]{3,2,1,0:T(8,128)}, u32[]{:S(2)}, u32[]{:S(2)}) collective-permute-start(f32[8,1,16,256]{3,2,1,0:T(8,128)} %get-tuple-element.995), channel_id=1, source_target_pairs={{0,1},{1,2},{2,3},{3,4},{4,5},{5,6},{6,7},{8,9},{9,10},{10,11},{11... | collective-permute-start | bytes 393224 | tf_op jit(solution)/shard_map/while/body/eval_jaxpr/ppermute | solution.py:20
  163.3 1.3 collective-permute-start.3
  167.0 7.5 %multiply_add_fusion.7 = (f32[8,16,16,256]{3,2,1,0:T(8,128)}, f32[8,16,16,256]{3,2,1,0:T(8,128)}, f32[8,16,16,256]{3,2,1,0:T(8,128)}) fusion(f32[8,16,16,256]{3,2,1,0:T(8,128)S(1)} %copy.50, f32[]{:T(128)} %bitcast.98, f32[]{:T(128)} %bitcast.99, f32[8,16,16,256]{3,2,1,0:T(8,128)} %get-tuple-element.1066, f32[16,16,256]{2,1,0:T(8,128)S(1)} %get-tuple-element.991, ...), kind=kLoop, calls=%fused_computation.69.clone.1 | loop fusion | flops 14155776 | bytes 14417929 | tf_op jit(solution)/shard_map/while/body/eval_jaxpr/add | solution.py:130
  174.4 1.6 copy.50
  176.7 6.7 %collective-permute-start.2 = (f32[8,1,16,256]{3,2,1,0:T(8,128)}, f32[8,1,16,256]{3,2,1,0:T(8,128)}, u32[]{:S(2)}, u32[]{:S(2)}) collective-permute-start(f32[8,1,16,256]{3,2,1,0:T(8,128)} %get-tuple-element.995), channel_id=1, source_target_pairs={{0,1},{1,2},{2,3},{3,4},{4,5},{5,6},{6,7},{8,9},{9,10},{10,11},{11... | collective-permute-start | bytes 393224 | tf_op jit(solution)/shard_map/while/body/eval_jaxpr/ppermute | solution.py:20
  183.4 1.3 collective-permute-start.3
  187.1 7.5 %multiply_add_fusion.7 = (f32[8,16,16,256]{3,2,1,0:T(8,128)}, f32[8,16,16,256]{3,2,1,0:T(8,128)}, f32[8,16,16,256]{3,2,1,0:T(8,128)}) fusion(f32[8,16,16,256]{3,2,1,0:T(8,128)S(1)} %copy.50, f32[]{:T(128)} %bitcast.98, f32[]{:T(128)} %bitcast.99, f32[8,16,16,256]{3,2,1,0:T(8,128)} %get-tuple-element.1066, f32[16,16,256]{2,1,0:T(8,128)S(1)} %get-tuple-element.991, ...), kind=kLoop, calls=%fused_computation.69.clone.1 | loop fusion | flops 14155776 | bytes 14417929 | tf_op jit(solution)/shard_map/while/body/eval_jaxpr/add | solution.py:130
  194.5 1.6 copy.50
  196.8 5.8 %collective-permute-start.2 = (f32[8,1,16,256]{3,2,1,0:T(8,128)}, f32[8,1,16,256]{3,2,1,0:T(8,128)}, u32[]{:S(2)}, u32[]{:S(2)}) collective-permute-start(f32[8,1,16,256]{3,2,1,0:T(8,128)} %get-tuple-element.995), channel_id=1, source_target_pairs={{0,1},{1,2},{2,3},{3,4},{4,5},{5,6},{6,7},{8,9},{9,10},{10,11},{11... | collective-permute-start | bytes 393224 | tf_op jit(solution)/shard_map/while/body/eval_jaxpr/ppermute | solution.py:20
  202.6 1.3 collective-permute-start.3
  206.3 7.5 %multiply_add_fusion.7 = (f32[8,16,16,256]{3,2,1,0:T(8,128)}, f32[8,16,16,256]{3,2,1,0:T(8,128)}, f32[8,16,16,256]{3,2,1,0:T(8,128)}) fusion(f32[8,16,16,256]{3,2,1,0:T(8,128)S(1)} %copy.50, f32[]{:T(128)} %bitcast.98, f32[]{:T(128)} %bitcast.99, f32[8,16,16,256]{3,2,1,0:T(8,128)} %get-tuple-element.1066, f32[16,16,256]{2,1,0:T(8,128)S(1)} %get-tuple-element.991, ...), kind=kLoop, calls=%fused_computation.69.clone.1 | loop fusion | flops 14155776 | bytes 14417929 | tf_op jit(solution)/shard_map/while/body/eval_jaxpr/add | solution.py:130
  213.7 4.9 %broadcast_multiply_fusion.4 = (f32[8,16,16,256]{3,2,1,0:T(8,128)}, f32[8,16,16,256]{3,2,1,0:T(8,128)}) fusion(f32[16,16,256]{2,1,0:T(8,128)} %add.631, f32[8,16,16,256]{3,2,1,0:T(8,128)} %get-tuple-element.571, f32[8,16,16,256]{3,2,1,0:T(8,128)} %get-tuple-element.572), kind=kLoop, calls=%fused_computation.180 | loop fusion | flops 1572864 | bytes 8650752 | tf_op jit(solution)/shard_map/mul | solution.py:122
  218.7 75.9 %while.65 = (s32[]{:T(128)}, f32[8,16,16,256]{3,2,1,0:T(8,128)}, f32[8,16,16,256]{3,2,1,0:T(8,128)}, f32[8,16,16,256]{3,2,1,0:T(8,128)}, f32[16,16,256]{2,1,0:T(...) while((s32[]{:T(128)}, f32[8,16,16,256]{3,2,1,0:T(8,128)}, ...), condition=%wide.region_7.8_spmd.clone.clone, body=%wide.region_6.7_spmd.sunk.clone.clone.sunk | while | flops 14811139 | bytes 23068904 | solution.py:133
  218.7 1.6 copy.51
  221.0 5.8 %collective-permute-start.4 = (f32[8,1,16,256]{3,2,1,0:T(8,128)}, f32[8,1,16,256]{3,2,1,0:T(8,128)}, u32[]{:S(2)}, u32[]{:S(2)}) collective-permute-start(f32[8,1,16,256]{3,2,1,0:T(8,128)} %get-tuple-element.1013), channel_id=1, source_target_pairs={{0,1},{1,2},{2,3},{3,4},{4,5},{5,6},{6,7},{8,9},{9,10},{10,11},{11... | collective-permute-start | bytes 393224 | tf_op jit(solution)/shard_map/while/body/eval_jaxpr/ppermute | solution.py:20
  230.3 7.0 %multiply_add_fusion.8 = (f32[8,16,16,256]{3,2,1,0:T(8,128)}, f32[8,16,16,256]{3,2,1,0:T(8,128)}, f32[8,16,16,256]{3,2,1,0:T(8,128)}) fusion(f32[8,16,16,256]{3,2,1,0:T(8,128)S(1)} %copy.51, f32[]{:T(128)} %bitcast.100, f32[]{:T(128)} %bitcast.101, f32[8,16,16,256]{3,2,1,0:T(8,128)} %get-tuple-element.1099, ...), kind=kLoop, calls=%fused_computation.110.clone.1 | loop fusion | flops 14155776 | bytes 14417929 | tf_op jit(solution)/shard_map/while/body/eval_jaxpr/add | solution.py:130
  237.3 1.6 copy.51
  239.6 5.8 %collective-permute-start.4 = (f32[8,1,16,256]{3,2,1,0:T(8,128)}, f32[8,1,16,256]{3,2,1,0:T(8,128)}, u32[]{:S(2)}, u32[]{:S(2)}) collective-permute-start(f32[8,1,16,256]{3,2,1,0:T(8,128)} %get-tuple-element.1013), channel_id=1, source_target_pairs={{0,1},{1,2},{2,3},{3,4},{4,5},{5,6},{6,7},{8,9},{9,10},{10,11},{11... | collective-permute-start | bytes 393224 | tf_op jit(solution)/shard_map/while/body/eval_jaxpr/ppermute | solution.py:20
  249.1 7.3 %multiply_add_fusion.8 = (f32[8,16,16,256]{3,2,1,0:T(8,128)}, f32[8,16,16,256]{3,2,1,0:T(8,128)}, f32[8,16,16,256]{3,2,1,0:T(8,128)}) fusion(f32[8,16,16,256]{3,2,1,0:T(8,128)S(1)} %copy.51, f32[]{:T(128)} %bitcast.100, f32[]{:T(128)} %bitcast.101, f32[8,16,16,256]{3,2,1,0:T(8,128)} %get-tuple-element.1099, ...), kind=kLoop, calls=%fused_computation.110.clone.1 | loop fusion | flops 14155776 | bytes 14417929 | tf_op jit(solution)/shard_map/while/body/eval_jaxpr/add | solution.py:130
  256.4 1.6 copy.51
  258.7 5.8 %collective-permute-start.4 = (f32[8,1,16,256]{3,2,1,0:T(8,128)}, f32[8,1,16,256]{3,2,1,0:T(8,128)}, u32[]{:S(2)}, u32[]{:S(2)}) collective-permute-start(f32[8,1,16,256]{3,2,1,0:T(8,128)} %get-tuple-element.1013), channel_id=1, source_target_pairs={{0,1},{1,2},{2,3},{3,4},{4,5},{5,6},{6,7},{8,9},{9,10},{10,11},{11... | collective-permute-start | bytes 393224 | tf_op jit(solution)/shard_map/while/body/eval_jaxpr/ppermute | solution.py:20
  268.1 7.3 %multiply_add_fusion.8 = (f32[8,16,16,256]{3,2,1,0:T(8,128)}, f32[8,16,16,256]{3,2,1,0:T(8,128)}, f32[8,16,16,256]{3,2,1,0:T(8,128)}) fusion(f32[8,16,16,256]{3,2,1,0:T(8,128)S(1)} %copy.51, f32[]{:T(128)} %bitcast.100, f32[]{:T(128)} %bitcast.101, f32[8,16,16,256]{3,2,1,0:T(8,128)} %get-tuple-element.1099, ...), kind=kLoop, calls=%fused_computation.110.clone.1 | loop fusion | flops 14155776 | bytes 14417929 | tf_op jit(solution)/shard_map/while/body/eval_jaxpr/add | solution.py:130
  275.5 1.6 copy.51
  277.8 5.8 %collective-permute-start.4 = (f32[8,1,16,256]{3,2,1,0:T(8,128)}, f32[8,1,16,256]{3,2,1,0:T(8,128)}, u32[]{:S(2)}, u32[]{:S(2)}) collective-permute-start(f32[8,1,16,256]{3,2,1,0:T(8,128)} %get-tuple-element.1013), channel_id=1, source_target_pairs={{0,1},{1,2},{2,3},{3,4},{4,5},{5,6},{6,7},{8,9},{9,10},{10,11},{11... | collective-permute-start | bytes 393224 | tf_op jit(solution)/shard_map/while/body/eval_jaxpr/ppermute | solution.py:20
  287.2 7.3 %multiply_add_fusion.8 = (f32[8,16,16,256]{3,2,1,0:T(8,128)}, f32[8,16,16,256]{3,2,1,0:T(8,128)}, f32[8,16,16,256]{3,2,1,0:T(8,128)}) fusion(f32[8,16,16,256]{3,2,1,0:T(8,128)S(1)} %copy.51, f32[]{:T(128)} %bitcast.100, f32[]{:T(128)} %bitcast.101, f32[8,16,16,256]{3,2,1,0:T(8,128)} %get-tuple-element.1099, ...), kind=kLoop, calls=%fused_computation.110.clone.1 | loop fusion | flops 14155776 | bytes 14417929 | tf_op jit(solution)/shard_map/while/body/eval_jaxpr/add | solution.py:130
  294.5 2.7 add.632
  297.3 5.2 %collective-permute-start.10 = (f32[8,1,16,256]{3,2,1,0:T(8,128)S(1)}, f32[8,1,16,256]{3,2,1,0:T(8,128)S(1)}, u32[]{:S(2)}, u32[]{:S(2)}) collective-permute-start(f32[8,1,16,256]{3,2,1,0:T(8,128)S(1)} %get-tuple-element.818), channel_id=1, source_target_pairs={{0,1},{1,2},{2,3},{3,4},{4,5},{5,6},{6,7},{8,9},{9,10},{10,11},{11... | collective-permute-start | bytes 393224 | tf_op jit(solution)/shard_map/ppermute | solution.py:20
  302.5 1.3 collective-permute-start.11
  303.8 1.9 collective-permute-done.11
  307.5 3.2 fusion.107
  310.7 89.1 %all-reduce.20.cloned.1.call-done = f32[8,16,16,256]{3,2,1,0:T(8,128)} async-done(((f32[8,16,16,256]{3,2,1,0:T(8,128)}), f32[8,16,16,256]{3,2,1,0:T(8,128)}) %all-reduce.20.cloned.1.call-update) | async-done | bytes 2097168 | tf_op jit(solution)/shard_map/psum | solution.py:150
  399.8 1.9 constant_dynamic-slice_fusion
  (154 shorter events, 48.2 us)
Async XLA Ops:
  6.5 50.8 %all-gather.2.cloned.1.call-start = ((), (), s32[]{:S(2)}) async-start(), calls=%async_computation | async-start | bytes 2621440 | tf_op jit(solution)/shard_map/all_gather | solution.py:102
  7.3 392.5 %all-reduce.20.cloned.1.call-start = ((), (), s32[]{:S(2)}) async-start(), calls=%async_computation.1 | async-start | bytes 4194304 | tf_op jit(solution)/shard_map/psum | solution.py:150
  9.0 60.8 %copy-start = (f32[1,16,16,256]{3,2,1,0:T(8,128)}, f32[1,16,16,256]{3,2,1,0:T(8,128)S(1)}, u32[]{:S(2)}) copy-start(f32[1,16,16,256]{3,2,1,0:T(8,128)S(1)} %get-tuple-element.823) | copy-start | bytes 786436
  59.3 5.2 %copy-start.13 = (s32[1,8]{1,0:T(1,128)S(1)}, s32[1,8]{1,0:T(1,128)}, u32[]{:S(2)}) copy-start(s32[1,8]{1,0:T(1,128)} %param.16) | copy-start | bytes 100
  59.3 5.2 %copy-start.14 = (f32[1,8]{1,0:T(1,128)S(1)}, f32[1,8]{1,0:T(1,128)}, u32[]{:S(2)}) copy-start(f32[1,8]{1,0:T(1,128)} %param.17) | copy-start | bytes 100
  60.2 7.9 %collective-permute-start.6 = (f32[9,2,16,256]{3,2,1,0:T(8,128)}, f32[9,2,16,256]{3,2,1,0:T(8,128)S(1)}, u32[]{:S(2)}, u32[]{:S(2)}) collective-permute-start(f32[9,2,16,256]{3,2,1,0:T(8,128)} %get-tuple-element.817), channel_id=1, source_target_pairs={{1,0},{2,1},{3,2},{4,3},{5,4},{6,5},{7,6},{9,8},{10,9},{11,10},{12... | collective-permute-start | bytes 884744 | tf_op jit(solution)/shard_map/ppermute | solution.py:22
  61.4 6.7 %collective-permute-start.7 = (f32[9,2,16,256]{3,2,1,0:T(8,128)}, f32[9,2,16,256]{3,2,1,0:T(8,128)S(1)}, u32[]{:S(2)}, u32[]{:S(2)}) collective-permute-start(f32[9,2,16,256]{3,2,1,0:T(8,128)} %get-tuple-element.816), channel_id=1, source_target_pairs={{0,1},{1,2},{2,3},{3,4},{4,5},{5,6},{6,7},{8,9},{9,10},{10,11},{11... | collective-permute-start | bytes 884744 | tf_op jit(solution)/shard_map/ppermute | solution.py:20
  68.1 2.6 copy-start.2
  68.1 0.8 copy-start.4
  69.9 0.8 copy-start.15
  69.9 0.8 copy-start.16
  71.7 5.9 %collective-permute-start = (f32[1,1,16,256]{3,2,1,0:T(8,128)S(1)}, f32[1,1,16,256]{3,2,1,0:T(8,128)S(1)}, u32[]{:S(2)}, u32[]{:S(2)}) collective-permute-start(f32[1,1,16,256]{3,2,1,0:T(8,128)S(1)} %get-tuple-element.979), channel_id=1, source_target_pairs={{0,1},{1,2},{2,3},{3,4},{4,5},{5,6},{6,7},{8,9},{9,10},{10,11},{11... | collective-permute-start | bytes 49160 | tf_op jit(solution)/shard_map/while/body/eval_jaxpr/ppermute | solution.py:20
  75.0 5.0 %collective-permute-start.1 = (f32[1,1,16,256]{3,2,1,0:T(8,128)S(1)}, f32[1,1,16,256]{3,2,1,0:T(8,128)S(1)}, u32[]{:S(2)}, u32[]{:S(2)}) collective-permute-start(f32[1,1,16,256]{3,2,1,0:T(8,128)S(1)} %get-tuple-element.980), channel_id=1, source_target_pairs={{1,0},{2,1},{3,2},{4,3},{5,4},{6,5},{7,6},{9,8},{10,9},{11,10},{12... | collective-permute-start | bytes 49160 | tf_op jit(solution)/shard_map/while/body/eval_jaxpr/ppermute | solution.py:22
  84.4 7.0 %collective-permute-start = (f32[1,1,16,256]{3,2,1,0:T(8,128)S(1)}, f32[1,1,16,256]{3,2,1,0:T(8,128)S(1)}, u32[]{:S(2)}, u32[]{:S(2)}) collective-permute-start(f32[1,1,16,256]{3,2,1,0:T(8,128)S(1)} %get-tuple-element.979), channel_id=1, source_target_pairs={{0,1},{1,2},{2,3},{3,4},{4,5},{5,6},{6,7},{8,9},{9,10},{10,11},{11... | collective-permute-start | bytes 49160 | tf_op jit(solution)/shard_map/while/body/eval_jaxpr/ppermute | solution.py:20
  88.8 3.3 collective-permute-start.1
  96.7 8.6 %collective-permute-start = (f32[1,1,16,256]{3,2,1,0:T(8,128)S(1)}, f32[1,1,16,256]{3,2,1,0:T(8,128)S(1)}, u32[]{:S(2)}, u32[]{:S(2)}) collective-permute-start(f32[1,1,16,256]{3,2,1,0:T(8,128)S(1)} %get-tuple-element.979), channel_id=1, source_target_pairs={{0,1},{1,2},{2,3},{3,4},{4,5},{5,6},{6,7},{8,9},{9,10},{10,11},{11... | collective-permute-start | bytes 49160 | tf_op jit(solution)/shard_map/while/body/eval_jaxpr/ppermute | solution.py:20
  102.7 3.1 collective-permute-start.1
  110.3 7.4 %collective-permute-start = (f32[1,1,16,256]{3,2,1,0:T(8,128)S(1)}, f32[1,1,16,256]{3,2,1,0:T(8,128)S(1)}, u32[]{:S(2)}, u32[]{:S(2)}) collective-permute-start(f32[1,1,16,256]{3,2,1,0:T(8,128)S(1)} %get-tuple-element.979), channel_id=1, source_target_pairs={{0,1},{1,2},{2,3},{3,4},{4,5},{5,6},{6,7},{8,9},{9,10},{10,11},{11... | collective-permute-start | bytes 49160 | tf_op jit(solution)/shard_map/while/body/eval_jaxpr/ppermute | solution.py:20
  115.2 3.1 collective-permute-start.1
  122.9 8.9 %collective-permute-start.8 = (f32[1,1,16,256]{3,2,1,0:T(8,128)S(1)}, f32[1,1,16,256]{3,2,1,0:T(8,128)S(1)}, u32[]{:S(2)}, u32[]{:S(2)}) collective-permute-start(f32[1,1,16,256]{3,2,1,0:T(8,128)S(1)} %get-tuple-element.831), channel_id=1, source_target_pairs={{0,1},{1,2},{2,3},{3,4},{4,5},{5,6},{6,7},{8,9},{9,10},{10,11},{11... | collective-permute-start | bytes 49160 | tf_op jit(solution)/shard_map/ppermute | solution.py:20
  127.7 4.1 collective-permute-start.9
  131.9 1.4 copy-start.1
  131.9 1.4 copy-start.3
  131.9 1.4 copy-start.5
  139.6 8.1 %collective-permute-start.2 = (f32[8,1,16,256]{3,2,1,0:T(8,128)}, f32[8,1,16,256]{3,2,1,0:T(8,128)}, u32[]{:S(2)}, u32[]{:S(2)}) collective-permute-start(f32[8,1,16,256]{3,2,1,0:T(8,128)} %get-tuple-element.995), channel_id=1, source_target_pairs={{0,1},{1,2},{2,3},{3,4},{4,5},{5,6},{6,7},{8,9},{9,10},{10,11},{11... | collective-permute-start | bytes 393224 | tf_op jit(solution)/shard_map/while/body/eval_jaxpr/ppermute | solution.py:20
  144.0 3.8 collective-permute-start.3
  157.3 9.7 %collective-permute-start.2 = (f32[8,1,16,256]{3,2,1,0:T(8,128)}, f32[8,1,16,256]{3,2,1,0:T(8,128)}, u32[]{:S(2)}, u32[]{:S(2)}) collective-permute-start(f32[8,1,16,256]{3,2,1,0:T(8,128)} %get-tuple-element.995), channel_id=1, source_target_pairs={{0,1},{1,2},{2,3},{3,4},{4,5},{5,6},{6,7},{8,9},{9,10},{10,11},{11... | collective-permute-start | bytes 393224 | tf_op jit(solution)/shard_map/while/body/eval_jaxpr/ppermute | solution.py:20
  163.3 3.6 collective-permute-start.3
  176.7 10.3 %collective-permute-start.2 = (f32[8,1,16,256]{3,2,1,0:T(8,128)}, f32[8,1,16,256]{3,2,1,0:T(8,128)}, u32[]{:S(2)}, u32[]{:S(2)}) collective-permute-start(f32[8,1,16,256]{3,2,1,0:T(8,128)} %get-tuple-element.995), channel_id=1, source_target_pairs={{0,1},{1,2},{2,3},{3,4},{4,5},{5,6},{6,7},{8,9},{9,10},{10,11},{11... | collective-permute-start | bytes 393224 | tf_op jit(solution)/shard_map/while/body/eval_jaxpr/ppermute | solution.py:20
  183.4 3.6 collective-permute-start.3
  196.8 9.4 %collective-permute-start.2 = (f32[8,1,16,256]{3,2,1,0:T(8,128)}, f32[8,1,16,256]{3,2,1,0:T(8,128)}, u32[]{:S(2)}, u32[]{:S(2)}) collective-permute-start(f32[8,1,16,256]{3,2,1,0:T(8,128)} %get-tuple-element.995), channel_id=1, source_target_pairs={{0,1},{1,2},{2,3},{3,4},{4,5},{5,6},{6,7},{8,9},{9,10},{10,11},{11... | collective-permute-start | bytes 393224 | tf_op jit(solution)/shard_map/while/body/eval_jaxpr/ppermute | solution.py:20
  202.6 3.6 collective-permute-start.3
  221.0 9.3 %collective-permute-start.4 = (f32[8,1,16,256]{3,2,1,0:T(8,128)}, f32[8,1,16,256]{3,2,1,0:T(8,128)}, u32[]{:S(2)}, u32[]{:S(2)}) collective-permute-start(f32[8,1,16,256]{3,2,1,0:T(8,128)} %get-tuple-element.1013), channel_id=1, source_target_pairs={{0,1},{1,2},{2,3},{3,4},{4,5},{5,6},{6,7},{8,9},{9,10},{10,11},{11... | collective-permute-start | bytes 393224 | tf_op jit(solution)/shard_map/while/body/eval_jaxpr/ppermute | solution.py:20
  226.8 3.6 collective-permute-start.5
  239.6 9.4 %collective-permute-start.4 = (f32[8,1,16,256]{3,2,1,0:T(8,128)}, f32[8,1,16,256]{3,2,1,0:T(8,128)}, u32[]{:S(2)}, u32[]{:S(2)}) collective-permute-start(f32[8,1,16,256]{3,2,1,0:T(8,128)} %get-tuple-element.1013), channel_id=1, source_target_pairs={{0,1},{1,2},{2,3},{3,4},{4,5},{5,6},{6,7},{8,9},{9,10},{10,11},{11... | collective-permute-start | bytes 393224 | tf_op jit(solution)/shard_map/while/body/eval_jaxpr/ppermute | solution.py:20
  245.5 3.6 collective-permute-start.5
  258.7 9.4 %collective-permute-start.4 = (f32[8,1,16,256]{3,2,1,0:T(8,128)}, f32[8,1,16,256]{3,2,1,0:T(8,128)}, u32[]{:S(2)}, u32[]{:S(2)}) collective-permute-start(f32[8,1,16,256]{3,2,1,0:T(8,128)} %get-tuple-element.1013), channel_id=1, source_target_pairs={{0,1},{1,2},{2,3},{3,4},{4,5},{5,6},{6,7},{8,9},{9,10},{10,11},{11... | collective-permute-start | bytes 393224 | tf_op jit(solution)/shard_map/while/body/eval_jaxpr/ppermute | solution.py:20
  264.6 3.6 collective-permute-start.5
  277.8 9.4 %collective-permute-start.4 = (f32[8,1,16,256]{3,2,1,0:T(8,128)}, f32[8,1,16,256]{3,2,1,0:T(8,128)}, u32[]{:S(2)}, u32[]{:S(2)}) collective-permute-start(f32[8,1,16,256]{3,2,1,0:T(8,128)} %get-tuple-element.1013), channel_id=1, source_target_pairs={{0,1},{1,2},{2,3},{3,4},{4,5},{5,6},{6,7},{8,9},{9,10},{10,11},{11... | collective-permute-start | bytes 393224 | tf_op jit(solution)/shard_map/while/body/eval_jaxpr/ppermute | solution.py:20
  283.6 3.6 collective-permute-start.5
  297.3 6.5 %collective-permute-start.10 = (f32[8,1,16,256]{3,2,1,0:T(8,128)S(1)}, f32[8,1,16,256]{3,2,1,0:T(8,128)S(1)}, u32[]{:S(2)}, u32[]{:S(2)}) collective-permute-start(f32[8,1,16,256]{3,2,1,0:T(8,128)S(1)} %get-tuple-element.818), channel_id=1, source_target_pairs={{0,1},{1,2},{2,3},{3,4},{4,5},{5,6},{6,7},{8,9},{9,10},{10,11},{11... | collective-permute-start | bytes 393224 | tf_op jit(solution)/shard_map/ppermute | solution.py:20
  302.5 3.2 collective-permute-start.11
  306.1 1.0 copy-start.6
  306.1 1.0 copy-start.7
  306.1 1.1 copy-start.8
  306.1 1.2 copy-start.9
  306.1 1.2 copy-start.10
  306.1 1.3 copy-start.11
  306.1 1.4 copy-start.12
Sparse Core Ops, SparseCore 0:
  8.9 48.3 all-gather.1
  310.8 88.8 all-reduce.19
where the time goes:
time: 410 us; the launch traced here: 408 us
  waiting for transfers between devices  144 us (35%)
  other arithmetic  110 us (27%)
  starting transfers between devices  97.2 us (24%)
  local copies, waits for them, and re-layouts  42.9 us (10%)
  between operations  13.8 us (3%)
    psum x1, waiting for transfers between devices, shards(): total = lax.psum(partial_value, 'test')  89.1 us
    ppermute x15, starting transfers between devices, with_halo(): lax.ppermute(tail, axis, [(i, (i + 1) % count) for i in range(ends)])  77.9 us
    add x12, other arithmetic, sweep(): direction = keep_table[turn] * direction + push_table[turn] * residual  72.8 us
    all_gather x1, waiting for transfers between devices, shards(): columns = lax.all_gather(panel, 'test', axis=0, tiled=True)  48.2 us
    ppermute x15, starting transfers between devices, with_halo(): lax.ppermute(head, axis, [((i + 1) % count, i) for i in range(ends)])  19.3 us
    while x12, local copies, waits for them, and re-layouts  16.5 us
    dynamic_slice x24, local copies, waits for them, and re-layouts, sweep(): direction = keep_table[turn] * direction + push_table[turn] * residual  15.1 us
    mul x3, other arithmetic, solve(): direction = right_side * first  10.7 us
  transfers between devices with their start and end apart: 32, of which 8 were waited for; matrix products, arithmetic and copies ran while one was open for 8% of the time, Pallas kernels for 0%

commit v1 on v0

--- a/solution.py
+++ b/solution.py
@@ -147,7 +147,9 @@
     adjoint_ext = rims(adjoint).reshape(tests_here, columns_all, slab + 2, rows_y, depth_z)
     contrib = jnp.sum(pairs(state_ext[:, None], adjoint_ext), axis=0)
     partial_value = -0.5 * perm[None] * contrib
-    total = lax.psum(partial_value, "test")
+    total = partial_value
+    for hop in (1, 2):
+        total = total + lax.ppermute(total, "test", [(dev, dev ^ hop) for dev in range(4)])
     share = panel.shape[0]
     owned = lax.dynamic_slice_in_dim(total, lax.axis_index("test") * share, share, 0)
     return owned

time: 410 us -> 463 us (1.13)
  waiting for transfers between devices: 144 us -> 193 us
    ppermute x0 -> x2, waiting for transfers between devices: none -> 138 us  [shards(): lax.ppermute(total, 'test', [(dev, dev ^ hop) for dev in range(4)])]
    psum x1 -> x0, waiting for transfers between devices: 89.1 us -> none  [shards(): total = lax.psum(partial_value, 'test')]
  transfers between devices with their start and end apart: 32 -> 33, of which waited for: 8 -> 9; matrix products, arithmetic and copies ran while one was open for 8% -> 7% of each run, Pallas kernels for 0% -> 0%
where the time goes in v1:
time: 463 us; the launch traced here: 459 us
  waiting for transfers between devices  193 us (42%)
  other arithmetic  112 us (24%)
  starting transfers between devices  98.4 us (21%)
  local copies, waits for them, and re-layouts  41.2 us (9%)
  between operations  13.8 us (3%)
    ppermute x2, waiting for transfers between devices, shards(): lax.ppermute(total, 'test', [(dev, dev ^ hop) for dev in range(4)])  138 us
    ppermute x15, starting transfers between devices, with_halo(): lax.ppermute(tail, axis, [(i, (i + 1) % count) for i in range(ends)])  77.8 us
    add x12, other arithmetic, sweep(): direction = keep_table[turn] * direction + push_table[turn] * residual  73.1 us
    all_gather x1, waiting for transfers between devices, shards(): columns = lax.all_gather(panel, 'test', axis=0, tiled=True)  48.3 us
    ppermute x15, starting transfers between devices, with_halo(): lax.ppermute(head, axis, [((i + 1) % count, i) for i in range(ends)])  19.3 us
    while x12, local copies, waits for them, and re-layouts  16.5 us
    dynamic_slice x24, local copies, waits for them, and re-layouts, sweep(): direction = keep_table[turn] * direction + push_table[turn] * residual  15.2 us
    mul x3, other arithmetic, solve(): direction = right_side * first  10.7 us
  transfers between devices with their start and end apart: 33, of which 9 were waited for; matrix products, arithmetic and copies ran while one was open for 7% of the time, Pallas kernels for 0%

profile of v1, /device:TPU:0, one launch (start us, length us, event | category | flops | bytes accessed | tf_op | source)
XLA Modules:
  0.0 458.5 jit_solution(1333180532528747897)
XLA Ops:
  7.3 1.7 broadcast_multiply_fusion.14
  9.0 48.3 %all-gather.2.cloned.1.call-done = f32[8,16,16,256]{3,2,1,0:T(8,128)} async-done(((f32[2,16,16,256]{3,2,1,0:T(8,128)}), f32[8,16,16,256]{3,2,1,0:T(8,128)}) %all-gather.2.cloned.1.call-update) | async-done | bytes 2097168 | tf_op jit(solution)/shard_map/all_gather | solution.py:102
  57.3 2.0 broadcast_multiply_fusion.6
  60.2 1.3 collective-permute-start.6
  61.5 3.0 collective-permute-start.7
  64.5 1.7 fusion.86
  66.3 1.8 broadcast_multiply_fusion.13
  70.7 51.2 %while.63 = (s32[]{:T(128)}, f32[1,16,16,256]{3,2,1,0:T(8,128)}, f32[1,16,16,256]{3,2,1,0:T(8,128)}, f32[1,16,16,256]{3,2,1,0:T(8,128)}, f32[16,16,256]{2,1,0:T(...) while((s32[]{:T(128)}, f32[1,16,16,256]{3,2,1,0:T(8,128)}, ...), condition=%wide.region_2.3_spmd.clone.clone, body=%wide.region_1.2_spmd.sunk.clone.clone.sunk | while | flops 2424835 | bytes 3637479 | solution.py:133
  71.7 3.3 collective-permute-start
  75.0 1.3 collective-permute-start.1
  77.6 2.4 collective-permute-done.1
  80.0 3.5 multiply_add_fusion.6
  84.5 4.4 collective-permute-start
  88.8 1.3 collective-permute-start.1
  92.1 3.6 multiply_add_fusion.6
  96.7 6.0 %collective-permute-start = (f32[1,1,16,256]{3,2,1,0:T(8,128)S(1)}, f32[1,1,16,256]{3,2,1,0:T(8,128)S(1)}, u32[]{:S(2)}, u32[]{:S(2)}) collective-permute-start(f32[1,1,16,256]{3,2,1,0:T(8,128)S(1)} %get-tuple-element.979), channel_id=1, source_target_pairs={{0,1},{1,2},{2,3},{3,4},{4,5},{5,6},{6,7},{8,9},{9,10},{10,11},{11... | collective-permute-start | bytes 49160 | tf_op jit(solution)/shard_map/while/body/eval_jaxpr/ppermute | solution.py:20
  102.7 1.3 collective-permute-start.1
  105.8 3.6 multiply_add_fusion.6
  110.4 4.8 %collective-permute-start = (f32[1,1,16,256]{3,2,1,0:T(8,128)S(1)}, f32[1,1,16,256]{3,2,1,0:T(8,128)S(1)}, u32[]{:S(2)}, u32[]{:S(2)}) collective-permute-start(f32[1,1,16,256]{3,2,1,0:T(8,128)S(1)} %get-tuple-element.979), channel_id=1, source_target_pairs={{0,1},{1,2},{2,3},{3,4},{4,5},{5,6},{6,7},{8,9},{9,10},{10,11},{11... | collective-permute-start | bytes 49160 | tf_op jit(solution)/shard_map/while/body/eval_jaxpr/ppermute | solution.py:20
  115.2 1.3 collective-permute-start.1
  118.3 3.6 multiply_add_fusion.6
  123.0 4.8 %collective-permute-start.8 = (f32[1,1,16,256]{3,2,1,0:T(8,128)S(1)}, f32[1,1,16,256]{3,2,1,0:T(8,128)S(1)}, u32[]{:S(2)}, u32[]{:S(2)}) collective-permute-start(f32[1,1,16,256]{3,2,1,0:T(8,128)S(1)} %get-tuple-element.831), channel_id=1, source_target_pairs={{0,1},{1,2},{2,3},{3,4},{4,5},{5,6},{6,7},{8,9},{9,10},{10,11},{11... | collective-permute-start | bytes 49160 | tf_op jit(solution)/shard_map/ppermute | solution.py:20
  127.8 1.3 collective-permute-start.9
  130.2 1.7 add.635
  132.0 1.4 broadcast_multiply_fusion.10
  133.3 3.9 broadcast_multiply_fusion.5
  137.3 76.5 %while.64 = (s32[]{:T(128)}, f32[8,16,16,256]{3,2,1,0:T(8,128)}, f32[8,16,16,256]{3,2,1,0:T(8,128)}, f32[8,16,16,256]{3,2,1,0:T(8,128)}, f32[16,16,256]{2,1,0:T(...) while((s32[]{:T(128)}, f32[8,16,16,256]{3,2,1,0:T(8,128)}, ...), condition=%wide.region_4.5_spmd.clone.clone, body=%wide.region_3.4_spmd.sunk.clone.clone.sunk | while | flops 14811139 | bytes 23068904 | solution.py:133
  137.3 1.6 copy.49
  139.6 4.5 collective-permute-start.2
  144.1 1.3 collective-permute-start.3
  147.9 7.1 %multiply_add_fusion.7 = (f32[8,16,16,256]{3,2,1,0:T(8,128)}, f32[8,16,16,256]{3,2,1,0:T(8,128)}, f32[8,16,16,256]{3,2,1,0:T(8,128)}) fusion(f32[8,16,16,256]{3,2,1,0:T(8,128)S(1)} %copy.49, f32[]{:T(128)} %bitcast.98, f32[]{:T(128)} %bitcast.99, f32[8,16,16,256]{3,2,1,0:T(8,128)} %get-tuple-element.1066, f32[16,16,256]{2,1,0:T(8,128)S(1)} %get-tuple-element.991, ...), kind=kLoop, calls=%fused_computation.69.clone.1 | loop fusion | flops 14155776 | bytes 14417929 | tf_op jit(solution)/shard_map/while/body/eval_jaxpr/add | solution.py:130
  155.0 1.6 copy.49
  157.3 6.1 %collective-permute-start.2 = (f32[8,1,16,256]{3,2,1,0:T(8,128)}, f32[8,1,16,256]{3,2,1,0:T(8,128)}, u32[]{:S(2)}, u32[]{:S(2)}) collective-permute-start(f32[8,1,16,256]{3,2,1,0:T(8,128)} %get-tuple-element.995), channel_id=1, source_target_pairs={{0,1},{1,2},{2,3},{3,4},{4,5},{5,6},{6,7},{8,9},{9,10},{10,11},{11... | collective-permute-start | bytes 393224 | tf_op jit(solution)/shard_map/while/body/eval_jaxpr/ppermute | solution.py:20
  163.4 1.3 collective-permute-start.3
  167.0 7.5 %multiply_add_fusion.7 = (f32[8,16,16,256]{3,2,1,0:T(8,128)}, f32[8,16,16,256]{3,2,1,0:T(8,128)}, f32[8,16,16,256]{3,2,1,0:T(8,128)}) fusion(f32[8,16,16,256]{3,2,1,0:T(8,128)S(1)} %copy.49, f32[]{:T(128)} %bitcast.98, f32[]{:T(128)} %bitcast.99, f32[8,16,16,256]{3,2,1,0:T(8,128)} %get-tuple-element.1066, f32[16,16,256]{2,1,0:T(8,128)S(1)} %get-tuple-element.991, ...), kind=kLoop, calls=%fused_computation.69.clone.1 | loop fusion | flops 14155776 | bytes 14417929 | tf_op jit(solution)/shard_map/while/body/eval_jaxpr/add | solution.py:130
  174.5 1.6 copy.49
  176.8 6.7 %collective-permute-start.2 = (f32[8,1,16,256]{3,2,1,0:T(8,128)}, f32[8,1,16,256]{3,2,1,0:T(8,128)}, u32[]{:S(2)}, u32[]{:S(2)}) collective-permute-start(f32[8,1,16,256]{3,2,1,0:T(8,128)} %get-tuple-element.995), channel_id=1, source_target_pairs={{0,1},{1,2},{2,3},{3,4},{4,5},{5,6},{6,7},{8,9},{9,10},{10,11},{11... | collective-permute-start | bytes 393224 | tf_op jit(solution)/shard_map/while/body/eval_jaxpr/ppermute | solution.py:20
  187.1 7.5 %multiply_add_fusion.7 = (f32[8,16,16,256]{3,2,1,0:T(8,128)}, f32[8,16,16,256]{3,2,1,0:T(8,128)}, f32[8,16,16,256]{3,2,1,0:T(8,128)}) fusion(f32[8,16,16,256]{3,2,1,0:T(8,128)S(1)} %copy.49, f32[]{:T(128)} %bitcast.98, f32[]{:T(128)} %bitcast.99, f32[8,16,16,256]{3,2,1,0:T(8,128)} %get-tuple-element.1066, f32[16,16,256]{2,1,0:T(8,128)S(1)} %get-tuple-element.991, ...), kind=kLoop, calls=%fused_computation.69.clone.1 | loop fusion | flops 14155776 | bytes 14417929 | tf_op jit(solution)/shard_map/while/body/eval_jaxpr/add | solution.py:130
  194.6 1.6 copy.49
  196.9 5.8 %collective-permute-start.2 = (f32[8,1,16,256]{3,2,1,0:T(8,128)}, f32[8,1,16,256]{3,2,1,0:T(8,128)}, u32[]{:S(2)}, u32[]{:S(2)}) collective-permute-start(f32[8,1,16,256]{3,2,1,0:T(8,128)} %get-tuple-element.995), channel_id=1, source_target_pairs={{0,1},{1,2},{2,3},{3,4},{4,5},{5,6},{6,7},{8,9},{9,10},{10,11},{11... | collective-permute-start | bytes 393224 | tf_op jit(solution)/shard_map/while/body/eval_jaxpr/ppermute | solution.py:20
  206.3 7.5 %multiply_add_fusion.7 = (f32[8,16,16,256]{3,2,1,0:T(8,128)}, f32[8,16,16,256]{3,2,1,0:T(8,128)}, f32[8,16,16,256]{3,2,1,0:T(8,128)}) fusion(f32[8,16,16,256]{3,2,1,0:T(8,128)S(1)} %copy.49, f32[]{:T(128)} %bitcast.98, f32[]{:T(128)} %bitcast.99, f32[8,16,16,256]{3,2,1,0:T(8,128)} %get-tuple-element.1066, f32[16,16,256]{2,1,0:T(8,128)S(1)} %get-tuple-element.991, ...), kind=kLoop, calls=%fused_computation.69.clone.1 | loop fusion | flops 14155776 | bytes 14417929 | tf_op jit(solution)/shard_map/while/body/eval_jaxpr/add | solution.py:130
  213.8 4.9 %broadcast_multiply_fusion.4 = (f32[8,16,16,256]{3,2,1,0:T(8,128)}, f32[8,16,16,256]{3,2,1,0:T(8,128)}) fusion(f32[16,16,256]{2,1,0:T(8,128)} %add.635, f32[8,16,16,256]{3,2,1,0:T(8,128)} %get-tuple-element.571, f32[8,16,16,256]{3,2,1,0:T(8,128)} %get-tuple-element.572), kind=kLoop, calls=%fused_computation.180 | loop fusion | flops 1572864 | bytes 8650752 | tf_op jit(solution)/shard_map/mul | solution.py:122
  218.7 76.2 %while.65 = (s32[]{:T(128)}, f32[8,16,16,256]{3,2,1,0:T(8,128)}, f32[8,16,16,256]{3,2,1,0:T(8,128)}, f32[8,16,16,256]{3,2,1,0:T(8,128)}, f32[16,16,256]{2,1,0:T(...) while((s32[]{:T(128)}, f32[8,16,16,256]{3,2,1,0:T(8,128)}, ...), condition=%wide.region_7.8_spmd.clone.clone, body=%wide.region_6.7_spmd.sunk.clone.clone.sunk | while | flops 14811139 | bytes 23068904 | solution.py:133
  218.7 1.6 copy.50
  221.1 5.8 %collective-permute-start.4 = (f32[8,1,16,256]{3,2,1,0:T(8,128)}, f32[8,1,16,256]{3,2,1,0:T(8,128)}, u32[]{:S(2)}, u32[]{:S(2)}) collective-permute-start(f32[8,1,16,256]{3,2,1,0:T(8,128)} %get-tuple-element.1013), channel_id=1, source_target_pairs={{0,1},{1,2},{2,3},{3,4},{4,5},{5,6},{6,7},{8,9},{9,10},{10,11},{11... | collective-permute-start | bytes 393224 | tf_op jit(solution)/shard_map/while/body/eval_jaxpr/ppermute | solution.py:20
  230.5 7.0 %multiply_add_fusion.8 = (f32[8,16,16,256]{3,2,1,0:T(8,128)}, f32[8,16,16,256]{3,2,1,0:T(8,128)}, f32[8,16,16,256]{3,2,1,0:T(8,128)}) fusion(f32[8,16,16,256]{3,2,1,0:T(8,128)S(1)} %copy.50, f32[]{:T(128)} %bitcast.100, f32[]{:T(128)} %bitcast.101, f32[8,16,16,256]{3,2,1,0:T(8,128)} %get-tuple-element.1099, ...), kind=kLoop, calls=%fused_computation.110.clone.1 | loop fusion | flops 14155776 | bytes 14417929 | tf_op jit(solution)/shard_map/while/body/eval_jaxpr/add | solution.py:130
  237.5 1.6 copy.50
  239.9 5.8 %collective-permute-start.4 = (f32[8,1,16,256]{3,2,1,0:T(8,128)}, f32[8,1,16,256]{3,2,1,0:T(8,128)}, u32[]{:S(2)}, u32[]{:S(2)}) collective-permute-start(f32[8,1,16,256]{3,2,1,0:T(8,128)} %get-tuple-element.1013), channel_id=1, source_target_pairs={{0,1},{1,2},{2,3},{3,4},{4,5},{5,6},{6,7},{8,9},{9,10},{10,11},{11... | collective-permute-start | bytes 393224 | tf_op jit(solution)/shard_map/while/body/eval_jaxpr/ppermute | solution.py:20
  249.3 7.4 %multiply_add_fusion.8 = (f32[8,16,16,256]{3,2,1,0:T(8,128)}, f32[8,16,16,256]{3,2,1,0:T(8,128)}, f32[8,16,16,256]{3,2,1,0:T(8,128)}) fusion(f32[8,16,16,256]{3,2,1,0:T(8,128)S(1)} %copy.50, f32[]{:T(128)} %bitcast.100, f32[]{:T(128)} %bitcast.101, f32[8,16,16,256]{3,2,1,0:T(8,128)} %get-tuple-element.1099, ...), kind=kLoop, calls=%fused_computation.110.clone.1 | loop fusion | flops 14155776 | bytes 14417929 | tf_op jit(solution)/shard_map/while/body/eval_jaxpr/add | solution.py:130
  256.7 1.6 copy.50
  259.0 5.8 %collective-permute-start.4 = (f32[8,1,16,256]{3,2,1,0:T(8,128)}, f32[8,1,16,256]{3,2,1,0:T(8,128)}, u32[]{:S(2)}, u32[]{:S(2)}) collective-permute-start(f32[8,1,16,256]{3,2,1,0:T(8,128)} %get-tuple-element.1013), channel_id=1, source_target_pairs={{0,1},{1,2},{2,3},{3,4},{4,5},{5,6},{6,7},{8,9},{9,10},{10,11},{11... | collective-permute-start | bytes 393224 | tf_op jit(solution)/shard_map/while/body/eval_jaxpr/ppermute | solution.py:20
  268.4 7.4 %multiply_add_fusion.8 = (f32[8,16,16,256]{3,2,1,0:T(8,128)}, f32[8,16,16,256]{3,2,1,0:T(8,128)}, f32[8,16,16,256]{3,2,1,0:T(8,128)}) fusion(f32[8,16,16,256]{3,2,1,0:T(8,128)S(1)} %copy.50, f32[]{:T(128)} %bitcast.100, f32[]{:T(128)} %bitcast.101, f32[8,16,16,256]{3,2,1,0:T(8,128)} %get-tuple-element.1099, ...), kind=kLoop, calls=%fused_computation.110.clone.1 | loop fusion | flops 14155776 | bytes 14417929 | tf_op jit(solution)/shard_map/while/body/eval_jaxpr/add | solution.py:130
  275.8 1.6 copy.50
  278.1 5.8 %collective-permute-start.4 = (f32[8,1,16,256]{3,2,1,0:T(8,128)}, f32[8,1,16,256]{3,2,1,0:T(8,128)}, u32[]{:S(2)}, u32[]{:S(2)}) collective-permute-start(f32[8,1,16,256]{3,2,1,0:T(8,128)} %get-tuple-element.1013), channel_id=1, source_target_pairs={{0,1},{1,2},{2,3},{3,4},{4,5},{5,6},{6,7},{8,9},{9,10},{10,11},{11... | collective-permute-start | bytes 393224 | tf_op jit(solution)/shard_map/while/body/eval_jaxpr/ppermute | solution.py:20
  287.6 7.4 %multiply_add_fusion.8 = (f32[8,16,16,256]{3,2,1,0:T(8,128)}, f32[8,16,16,256]{3,2,1,0:T(8,128)}, f32[8,16,16,256]{3,2,1,0:T(8,128)}) fusion(f32[8,16,16,256]{3,2,1,0:T(8,128)S(1)} %copy.50, f32[]{:T(128)} %bitcast.100, f32[]{:T(128)} %bitcast.101, f32[8,16,16,256]{3,2,1,0:T(8,128)} %get-tuple-element.1099, ...), kind=kLoop, calls=%fused_computation.110.clone.1 | loop fusion | flops 14155776 | bytes 14417929 | tf_op jit(solution)/shard_map/while/body/eval_jaxpr/add | solution.py:130
  294.9 2.7 add.636
  297.7 5.2 %collective-permute-start.10 = (f32[8,1,16,256]{3,2,1,0:T(8,128)S(1)}, f32[8,1,16,256]{3,2,1,0:T(8,128)S(1)}, u32[]{:S(2)}, u32[]{:S(2)}) collective-permute-start(f32[8,1,16,256]{3,2,1,0:T(8,128)S(1)} %get-tuple-element.818), channel_id=1, source_target_pairs={{0,1},{1,2},{2,3},{3,4},{4,5},{5,6},{6,7},{8,9},{9,10},{10,11},{11... | collective-permute-start | bytes 393224 | tf_op jit(solution)/shard_map/ppermute | solution.py:20
  302.8 1.3 collective-permute-start.11
  304.2 1.9 collective-permute-done.11
  307.9 2.3 fusion.107
  310.2 45.5 %collective-permute-done.12 = f32[8,16,16,256]{3,2,1,0:T(8,128)S(1)} collective-permute-done((f32[8,16,16,256]{3,2,1,0:T(8,128)S(1)}, f32[8,16,16,256]{3,2,1,0:T(8,128)S(1)}, u32[]{:S(2)}, u32[]{:S(2)}) %collective-permute-start.12) | collective-permute-done | bytes 2097184 | tf_op jit(solution)/shard_map/ppermute | solution.py:152
  356.2 1.3 collective-permute-start.13
  357.5 92.3 %collective-permute-done.13 = f32[8,16,16,256]{3,2,1,0:T(8,128)} collective-permute-done((f32[8,16,16,256]{3,2,1,0:T(8,128)S(1)}, f32[8,16,16,256]{3,2,1,0:T(8,128)}, u32[]{:S(2)}, u32[]{:S(2)}) %collective-permute-start.13) | collective-permute-done | bytes 2097184 | tf_op jit(solution)/shard_map/ppermute | solution.py:152
  449.8 1.9 dynamic-slice_add_fusion
  (156 shorter events, 51.4 us)
Async XLA Ops:
  6.5 50.8 %all-gather.2.cloned.1.call-start = ((), (), s32[]{:S(2)}) async-start(), calls=%async_computation | async-start | bytes 2621440 | tf_op jit(solution)/shard_map/all_gather | solution.py:102
  9.0 60.8 %copy-start = (f32[1,16,16,256]{3,2,1,0:T(8,128)}, f32[1,16,16,256]{3,2,1,0:T(8,128)S(1)}, u32[]{:S(2)}) copy-start(f32[1,16,16,256]{3,2,1,0:T(8,128)S(1)} %get-tuple-element.823) | copy-start | bytes 786436
  59.3 5.2 %copy-start.13 = (s32[1,8]{1,0:T(1,128)S(1)}, s32[1,8]{1,0:T(1,128)}, u32[]{:S(2)}) copy-start(s32[1,8]{1,0:T(1,128)} %param.16) | copy-start | bytes 100
  59.3 5.2 %copy-start.14 = (f32[1,8]{1,0:T(1,128)S(1)}, f32[1,8]{1,0:T(1,128)}, u32[]{:S(2)}) copy-start(f32[1,8]{1,0:T(1,128)} %param.17) | copy-start | bytes 100
  60.2 7.9 %collective-permute-start.6 = (f32[9,2,16,256]{3,2,1,0:T(8,128)}, f32[9,2,16,256]{3,2,1,0:T(8,128)S(1)}, u32[]{:S(2)}, u32[]{:S(2)}) collective-permute-start(f32[9,2,16,256]{3,2,1,0:T(8,128)} %get-tuple-element.817), channel_id=1, source_target_pairs={{1,0},{2,1},{3,2},{4,3},{5,4},{6,5},{7,6},{9,8},{10,9},{11,10},{12... | collective-permute-start | bytes 884744 | tf_op jit(solution)/shard_map/ppermute | solution.py:22
  61.5 6.6 %collective-permute-start.7 = (f32[9,2,16,256]{3,2,1,0:T(8,128)}, f32[9,2,16,256]{3,2,1,0:T(8,128)S(1)}, u32[]{:S(2)}, u32[]{:S(2)}) collective-permute-start(f32[9,2,16,256]{3,2,1,0:T(8,128)} %get-tuple-element.816), channel_id=1, source_target_pairs={{0,1},{1,2},{2,3},{3,4},{4,5},{5,6},{6,7},{8,9},{9,10},{10,11},{11... | collective-permute-start | bytes 884744 | tf_op jit(solution)/shard_map/ppermute | solution.py:20
  68.1 2.6 copy-start.2
  68.1 0.8 copy-start.4
  69.9 0.8 copy-start.15
  69.9 0.8 copy-start.16
  71.7 5.9 %collective-permute-start = (f32[1,1,16,256]{3,2,1,0:T(8,128)S(1)}, f32[1,1,16,256]{3,2,1,0:T(8,128)S(1)}, u32[]{:S(2)}, u32[]{:S(2)}) collective-permute-start(f32[1,1,16,256]{3,2,1,0:T(8,128)S(1)} %get-tuple-element.979), channel_id=1, source_target_pairs={{0,1},{1,2},{2,3},{3,4},{4,5},{5,6},{6,7},{8,9},{9,10},{10,11},{11... | collective-permute-start | bytes 49160 | tf_op jit(solution)/shard_map/while/body/eval_jaxpr/ppermute | solution.py:20
  75.0 5.0 %collective-permute-start.1 = (f32[1,1,16,256]{3,2,1,0:T(8,128)S(1)}, f32[1,1,16,256]{3,2,1,0:T(8,128)S(1)}, u32[]{:S(2)}, u32[]{:S(2)}) collective-permute-start(f32[1,1,16,256]{3,2,1,0:T(8,128)S(1)} %get-tuple-element.980), channel_id=1, source_target_pairs={{1,0},{2,1},{3,2},{4,3},{5,4},{6,5},{7,6},{9,8},{10,9},{11,10},{12... | collective-permute-start | bytes 49160 | tf_op jit(solution)/shard_map/while/body/eval_jaxpr/ppermute | solution.py:22
  84.5 7.0 %collective-permute-start = (f32[1,1,16,256]{3,2,1,0:T(8,128)S(1)}, f32[1,1,16,256]{3,2,1,0:T(8,128)S(1)}, u32[]{:S(2)}, u32[]{:S(2)}) collective-permute-start(f32[1,1,16,256]{3,2,1,0:T(8,128)S(1)} %get-tuple-element.979), channel_id=1, source_target_pairs={{0,1},{1,2},{2,3},{3,4},{4,5},{5,6},{6,7},{8,9},{9,10},{10,11},{11... | collective-permute-start | bytes 49160 | tf_op jit(solution)/shard_map/while/body/eval_jaxpr/ppermute | solution.py:20
  88.8 3.3 collective-permute-start.1
  96.7 8.6 %collective-permute-start = (f32[1,1,16,256]{3,2,1,0:T(8,128)S(1)}, f32[1,1,16,256]{3,2,1,0:T(8,128)S(1)}, u32[]{:S(2)}, u32[]{:S(2)}) collective-permute-start(f32[1,1,16,256]{3,2,1,0:T(8,128)S(1)} %get-tuple-element.979), channel_id=1, source_target_pairs={{0,1},{1,2},{2,3},{3,4},{4,5},{5,6},{6,7},{8,9},{9,10},{10,11},{11... | collective-permute-start | bytes 49160 | tf_op jit(solution)/shard_map/while/body/eval_jaxpr/ppermute | solution.py:20
  102.7 3.1 collective-permute-start.1
  110.4 7.4 %collective-permute-start = (f32[1,1,16,256]{3,2,1,0:T(8,128)S(1)}, f32[1,1,16,256]{3,2,1,0:T(8,128)S(1)}, u32[]{:S(2)}, u32[]{:S(2)}) collective-permute-start(f32[1,1,16,256]{3,2,1,0:T(8,128)S(1)} %get-tuple-element.979), channel_id=1, source_target_pairs={{0,1},{1,2},{2,3},{3,4},{4,5},{5,6},{6,7},{8,9},{9,10},{10,11},{11... | collective-permute-start | bytes 49160 | tf_op jit(solution)/shard_map/while/body/eval_jaxpr/ppermute | solution.py:20
  115.2 3.1 collective-permute-start.1
  123.0 8.9 %collective-permute-start.8 = (f32[1,1,16,256]{3,2,1,0:T(8,128)S(1)}, f32[1,1,16,256]{3,2,1,0:T(8,128)S(1)}, u32[]{:S(2)}, u32[]{:S(2)}) collective-permute-start(f32[1,1,16,256]{3,2,1,0:T(8,128)S(1)} %get-tuple-element.831), channel_id=1, source_target_pairs={{0,1},{1,2},{2,3},{3,4},{4,5},{5,6},{6,7},{8,9},{9,10},{10,11},{11... | collective-permute-start | bytes 49160 | tf_op jit(solution)/shard_map/ppermute | solution.py:20
  127.8 4.1 collective-permute-start.9
  131.9 1.4 copy-start.1
  131.9 1.4 copy-start.3
  131.9 1.4 copy-start.5
  139.6 8.0 %collective-permute-start.2 = (f32[8,1,16,256]{3,2,1,0:T(8,128)}, f32[8,1,16,256]{3,2,1,0:T(8,128)}, u32[]{:S(2)}, u32[]{:S(2)}) collective-permute-start(f32[8,1,16,256]{3,2,1,0:T(8,128)} %get-tuple-element.995), channel_id=1, source_target_pairs={{0,1},{1,2},{2,3},{3,4},{4,5},{5,6},{6,7},{8,9},{9,10},{10,11},{11... | collective-permute-start | bytes 393224 | tf_op jit(solution)/shard_map/while/body/eval_jaxpr/ppermute | solution.py:20
  144.1 3.8 collective-permute-start.3
  157.3 9.6 %collective-permute-start.2 = (f32[8,1,16,256]{3,2,1,0:T(8,128)}, f32[8,1,16,256]{3,2,1,0:T(8,128)}, u32[]{:S(2)}, u32[]{:S(2)}) collective-permute-start(f32[8,1,16,256]{3,2,1,0:T(8,128)} %get-tuple-element.995), channel_id=1, source_target_pairs={{0,1},{1,2},{2,3},{3,4},{4,5},{5,6},{6,7},{8,9},{9,10},{10,11},{11... | collective-permute-start | bytes 393224 | tf_op jit(solution)/shard_map/while/body/eval_jaxpr/ppermute | solution.py:20
  163.4 3.6 collective-permute-start.3
  176.8 10.3 %collective-permute-start.2 = (f32[8,1,16,256]{3,2,1,0:T(8,128)}, f32[8,1,16,256]{3,2,1,0:T(8,128)}, u32[]{:S(2)}, u32[]{:S(2)}) collective-permute-start(f32[8,1,16,256]{3,2,1,0:T(8,128)} %get-tuple-element.995), channel_id=1, source_target_pairs={{0,1},{1,2},{2,3},{3,4},{4,5},{5,6},{6,7},{8,9},{9,10},{10,11},{11... | collective-permute-start | bytes 393224 | tf_op jit(solution)/shard_map/while/body/eval_jaxpr/ppermute | solution.py:20
  183.5 3.6 collective-permute-start.3
  196.9 9.4 %collective-permute-start.2 = (f32[8,1,16,256]{3,2,1,0:T(8,128)}, f32[8,1,16,256]{3,2,1,0:T(8,128)}, u32[]{:S(2)}, u32[]{:S(2)}) collective-permute-start(f32[8,1,16,256]{3,2,1,0:T(8,128)} %get-tuple-element.995), channel_id=1, source_target_pairs={{0,1},{1,2},{2,3},{3,4},{4,5},{5,6},{6,7},{8,9},{9,10},{10,11},{11... | collective-permute-start | bytes 393224 | tf_op jit(solution)/shard_map/while/body/eval_jaxpr/ppermute | solution.py:20
  202.7 3.6 collective-permute-start.3
  221.1 9.4 %collective-permute-start.4 = (f32[8,1,16,256]{3,2,1,0:T(8,128)}, f32[8,1,16,256]{3,2,1,0:T(8,128)}, u32[]{:S(2)}, u32[]{:S(2)}) collective-permute-start(f32[8,1,16,256]{3,2,1,0:T(8,128)} %get-tuple-element.1013), channel_id=1, source_target_pairs={{0,1},{1,2},{2,3},{3,4},{4,5},{5,6},{6,7},{8,9},{9,10},{10,11},{11... | collective-permute-start | bytes 393224 | tf_op jit(solution)/shard_map/while/body/eval_jaxpr/ppermute | solution.py:20
  226.9 3.6 collective-permute-start.5
  239.9 9.4 %collective-permute-start.4 = (f32[8,1,16,256]{3,2,1,0:T(8,128)}, f32[8,1,16,256]{3,2,1,0:T(8,128)}, u32[]{:S(2)}, u32[]{:S(2)}) collective-permute-start(f32[8,1,16,256]{3,2,1,0:T(8,128)} %get-tuple-element.1013), channel_id=1, source_target_pairs={{0,1},{1,2},{2,3},{3,4},{4,5},{5,6},{6,7},{8,9},{9,10},{10,11},{11... | collective-permute-start | bytes 393224 | tf_op jit(solution)/shard_map/while/body/eval_jaxpr/ppermute | solution.py:20
  245.7 3.6 collective-permute-start.5
  259.0 9.4 %collective-permute-start.4 = (f32[8,1,16,256]{3,2,1,0:T(8,128)}, f32[8,1,16,256]{3,2,1,0:T(8,128)}, u32[]{:S(2)}, u32[]{:S(2)}) collective-permute-start(f32[8,1,16,256]{3,2,1,0:T(8,128)} %get-tuple-element.1013), channel_id=1, source_target_pairs={{0,1},{1,2},{2,3},{3,4},{4,5},{5,6},{6,7},{8,9},{9,10},{10,11},{11... | collective-permute-start | bytes 393224 | tf_op jit(solution)/shard_map/while/body/eval_jaxpr/ppermute | solution.py:20
  264.8 3.6 collective-permute-start.5
  278.1 9.4 %collective-permute-start.4 = (f32[8,1,16,256]{3,2,1,0:T(8,128)}, f32[8,1,16,256]{3,2,1,0:T(8,128)}, u32[]{:S(2)}, u32[]{:S(2)}) collective-permute-start(f32[8,1,16,256]{3,2,1,0:T(8,128)} %get-tuple-element.1013), channel_id=1, source_target_pairs={{0,1},{1,2},{2,3},{3,4},{4,5},{5,6},{6,7},{8,9},{9,10},{10,11},{11... | collective-permute-start | bytes 393224 | tf_op jit(solution)/shard_map/while/body/eval_jaxpr/ppermute | solution.py:20
  283.9 3.6 collective-permute-start.5
  297.7 6.5 %collective-permute-start.10 = (f32[8,1,16,256]{3,2,1,0:T(8,128)S(1)}, f32[8,1,16,256]{3,2,1,0:T(8,128)S(1)}, u32[]{:S(2)}, u32[]{:S(2)}) collective-permute-start(f32[8,1,16,256]{3,2,1,0:T(8,128)S(1)} %get-tuple-element.818), channel_id=1, source_target_pairs={{0,1},{1,2},{2,3},{3,4},{4,5},{5,6},{6,7},{8,9},{9,10},{10,11},{11... | collective-permute-start | bytes 393224 | tf_op jit(solution)/shard_map/ppermute | solution.py:20
  302.8 3.2 collective-permute-start.11
  306.4 1.0 copy-start.6
  306.4 1.0 copy-start.7
  306.4 1.1 copy-start.8
  306.5 1.2 copy-start.9
  306.5 1.2 copy-start.10
  306.5 1.3 copy-start.11
  306.5 1.4 copy-start.12
  310.1 45.6 %collective-permute-start.12 = (f32[8,16,16,256]{3,2,1,0:T(8,128)S(1)}, f32[8,16,16,256]{3,2,1,0:T(8,128)S(1)}, u32[]{:S(2)}, u32[]{:S(2)}) collective-permute-start(f32[8,16,16,256]{3,2,1,0:T(8,128)S(1)} %fusion.107), channel_id=1, source_target_pairs={{0,8},{8,0},{16,24},{24,16},{1,9},{9,1},{17,25},{25,17},{2,10},{10... | collective-permute-start | bytes 6291464 | tf_op jit(solution)/shard_map/ppermute | solution.py:152
  356.2 93.6 %collective-permute-start.13 = (f32[8,16,16,256]{3,2,1,0:T(8,128)S(1)}, f32[8,16,16,256]{3,2,1,0:T(8,128)}, u32[]{:S(2)}, u32[]{:S(2)}) collective-permute-start(f32[8,16,16,256]{3,2,1,0:T(8,128)S(1)} %add.642), channel_id=1, source_target_pairs={{0,16},{8,24},{16,0},{24,8},{1,17},{9,25},{17,1},{25,9},{2,18},{10... | collective-permute-start | bytes 6291464 | tf_op jit(solution)/shard_map/ppermute | solution.py:152
Sparse Core Ops, SparseCore 0:
  8.9 48.3 all-gather.1
